TPU v7x, 32 devices: a whole 2x2x4 slice. The times are simulated.
32 devices in a mesh: group: 2 (over y), seq: 8 (over z, x), chan: 2 (over core).
Axes of the slice: x: 2, y: 2, z: 4, core: 2. Of those that a mesh axis runs over, the one named last changes fastest.
Arguments:
- fresh: bfloat16 [2048, 3, 2048], P(('group', 'seq'), None, 'chan'), parts along dimension 0, may hold values from -6 to 6
- library: bfloat16 [8, 8, 2048], P('seq', None, 'chan'), may hold values from -6 to 6
- block_slot: int32 [8], replicated, may hold values from 0 to 7, each once
- prefix_blocks: int32 [16, 4], P('group'), parts along dimension 0, may hold values from 0 to 7, all different within a row
- short_taps: float32 [3, 3, 2048], P(None, None, 'chan'), may hold values from -4 to 4
- long_filter: float32 [1024, 2048], P('seq', 'chan'), may hold values from -2 to 2
- skip_gain: float32 [2048], P('chan'), may hold values from -6 to 6
Outputs:
- mixed: bfloat16 [2048, 2048], P(('group', 'seq'), 'chan'), parts along dimension 0
There are 2 independent parts, one for each index of `group`. A program takes and returns all parts, laid end to end along the dimension named above; an argument that names none is the same for every part. Nothing has to cross between parts.
Inputs may be any that keep to these rules, and one draw needn't show every extreme that they name: `block_slot`: each number appears once. `prefix_blocks`: every library block is named at least once; the four entries of a row differ.
All inputs are finite; a program needn't handle non-finite values.
Results may differ from a plain program's by a relative error of at most 0.008.
Values may be sent and summed in bfloat16 or wider, within the bound.
No kernel may reach another device: no remote copies, remote signals or barrier semaphores. Data moves between devices by JAX's collectives and lax.ppermute only.
A program may use at most 64 MiB of HBM per device.

v0:
```python
import math
import jax
import jax.numpy as jnp
from jax import lax
from jax.sharding import PartitionSpec as P

TAPS = 3
BLK = 8


def from_behind(shard, axis, by):
    count = lax.axis_size(axis)
    pairs = [(i, i + by) for i in range(count) if 0 <= i + by < count]
    return lax.ppermute(shard, axis, pairs)


def exact_dot(pattern, matrix, tensor):
    return jnp.einsum(pattern, matrix, tensor, precision=lax.Precision.HIGHEST)


def turn_angles(numbers, period):
    return (numbers % period).astype(jnp.float32) * (2.0 * math.pi / period)


def body(fresh, library, block_slot, prefix_blocks, short_taps, long_filter, skip_gain):
    row_count = fresh.shape[0]
    channels = fresh.shape[2]
    devices = lax.axis_size("seq")
    seq_index = lax.axis_index("seq")
    group_rows = row_count // devices
    period = 2 * row_count * devices
    block_ids = jnp.arange(devices, dtype=jnp.int32)
    mode_ids = jnp.arange(2 * devices, dtype=jnp.int32)
    coarse = turn_angles(mode_ids[:, None] * block_ids[None, :], 2 * devices)
    cos_q = jnp.cos(coarse)
    sin_q = jnp.sin(coarse)
    local_rows = seq_index * group_rows + jnp.arange(group_rows, dtype=jnp.int32)
    twist = turn_angles(mode_ids[:, None] * local_rows[None, :], period)
    twist_cos = jnp.cos(twist)[:, :, None]
    twist_sin = jnp.sin(twist)[:, :, None]
    row_ids = jnp.arange(row_count, dtype=jnp.int32)
    fine_angles = turn_angles(row_ids[:, None] * row_ids[None, :], row_count)
    cos_m = jnp.cos(fine_angles)
    sin_m = jnp.sin(fine_angles)
    first_modes = 2 * seq_index + jnp.arange(2, dtype=jnp.int32)
    back_twist = turn_angles(first_modes[:, None] * row_ids[None, :], period)
    back_cos = jnp.cos(back_twist)[:, :, None]
    back_sin = jnp.sin(back_twist)[:, :, None]

    def to_modes(column):
        real_part = exact_dot("kq,qgc->kgc", cos_q, column)
        imag_part = -exact_dot("kq,qgc->kgc", sin_q, column)
        return jnp.stack(
            [
                real_part * twist_cos + imag_part * twist_sin,
                imag_part * twist_cos - real_part * twist_sin,
            ]
        )

    def to_spectrum(spread):
        real_part = exact_dot("ki,jic->jkc", cos_m, spread[0]) + exact_dot(
            "ki,jic->jkc", sin_m, spread[1]
        )
        imag_part = exact_dot("ki,jic->jkc", cos_m, spread[1]) - exact_dot(
            "ki,jic->jkc", sin_m, spread[0]
        )
        return (real_part, imag_part)

    blocks_here = row_count // BLK
    flat_ids = prefix_blocks.reshape(-1)
    first_block = jnp.minimum(seq_index * blocks_here, flat_ids.shape[0] - blocks_here)
    own_ids = lax.dynamic_slice_in_dim(flat_ids, first_block, blocks_here)
    matches = own_ids[:, None] == jnp.arange(block_slot.shape[0], dtype=jnp.int32)[None, :]
    wanted = jnp.sum(jnp.where(matches, block_slot[None, :], 0), axis=1)
    shards = lax.all_gather(library, "seq", axis=0, tiled=True)
    picker = (wanted[:, None] == jnp.arange(shards.shape[0], dtype=jnp.int32)[None, :]).astype(
        jnp.bfloat16
    )
    gathered = jnp.einsum("bn,nlc->blc", picker, shards, preferred_element_type=jnp.float32)
    cached = gathered.reshape(row_count, channels).astype(jnp.bfloat16)
    values = jnp.where(seq_index < devices // 4, cached, fresh[:, 2])
    stacked = jnp.concatenate([fresh[:, :2], values[:, None]], axis=1)
    previous = from_behind(stacked[row_count - (TAPS - 1) :], "seq", 1)
    extended = jnp.concatenate([previous, stacked], axis=0)
    shortened = jnp.zeros((row_count, 3, channels), jnp.float32)
    for offset in range(TAPS):
        window_start = TAPS - 1 - offset
        shortened = shortened + short_taps[offset][None] * extended[
            window_start : window_start + row_count
        ].astype(jnp.float32)
    gating = shortened[:, 0]
    signal = shortened[:, 1] * shortened[:, 2]
    spread_signal = to_modes(
        lax.all_to_all(signal[None], "seq", split_axis=1, concat_axis=0, tiled=True)
    )
    spread_taps = to_modes(
        lax.all_to_all(long_filter[None], "seq", split_axis=1, concat_axis=0, tiled=True)
    )
    moved_signal, moved_taps = (
        lax.all_to_all(
            spread_signal.astype(jnp.bfloat16), "seq", split_axis=1, concat_axis=2, tiled=True
        ).astype(spread_signal.dtype),
        lax.all_to_all(
            spread_taps.astype(jnp.bfloat16), "seq", split_axis=1, concat_axis=2, tiled=True
        ).astype(spread_taps.dtype),
    )
    sig_real, sig_imag = to_spectrum(moved_signal)
    tap_real, tap_imag = to_spectrum(moved_taps)
    prod_real = sig_real * tap_real - sig_imag * tap_imag
    prod_imag = sig_real * tap_imag + sig_imag * tap_real
    back_real = exact_dot("ki,jic->jkc", cos_m, prod_real) - exact_dot(
        "ki,jic->jkc", sin_m, prod_imag
    )
    back_imag = exact_dot("ki,jic->jkc", cos_m, prod_imag) + exact_dot(
        "ki,jic->jkc", sin_m, prod_real
    )
    turned = jnp.stack(
        [back_real * back_cos - back_imag * back_sin, back_imag * back_cos + back_real * back_sin]
    )
    spread = lax.all_to_all(turned, "seq", split_axis=2, concat_axis=1, tiled=True)
    positions = (
        exact_dot("kq,kgc->qgc", cos_q, spread[0]) - exact_dot("kq,kgc->qgc", sin_q, spread[1])
    ) / period
    convolved = lax.all_to_all(positions, "seq", split_axis=0, concat_axis=1, tiled=True)[0]
    output = gating * (convolved + skip_gain[None, :] * signal)
    return output.astype(jnp.bfloat16)


def solution(mesh):
    return jax.shard_map(
        body,
        mesh=mesh,
        in_specs=(
            P(("group", "seq"), None, "chan"),
            P("seq", None, "chan"),
            P(),
            P("group", None),
            P(None, None, "chan"),
            P("seq", "chan"),
            P("chan"),
        ),
        out_specs=P(("group", "seq"), "chan"),
        check_vma=False,
    )
```

profile of v0, /device:TPU:0, one launch (start us, length us, event | category | flops | bytes accessed | tf_op | source)
XLA Modules:
  0.0 217.2 jit_solution(2624598276856022187)
XLA Ops:
  0.0 2.3 %broadcast_in_dim.12 = f32[1,128,1024]{2,0,1:T(1,128)} reshape(f32[128,1024]{1,0:T(8,128)} %param.12) | data formatting | bytes 1048576 | tf_op jit(solution)/shard_map/broadcast_in_dim | solution.py:97
  2.3 7.3 %all-to-all-start.2 = ((f32[1,128,1024]{2,0,1:T(1,128)}), f32[1,128,1024]{2,0,1:T(1,128)S(1)}, u32[]{:S(2)}, u32[]{:S(2)}) async-start(f32[1,128,1024]{2,0,1:T(1,128)} %broadcast_in_dim.12), calls=%async_computation.2 | async-start | bytes 1048576 | tf_op jit(solution)/shard_map/all_to_all | solution.py:97
  9.8 37.2 %all_gather.3 = bf16[8,8,1024]{2,1,0:T(8,128)(2,1)S(1)} all-gather(bf16[1,8,1024]{2,1,0:T(8,128)(2,1)S(1)} %copy-done.7), channel_id=1, replica_groups=mesh['group'=2,'seq'=8,'chan'=2] {'seq'}, dimensions={0}, use_global_device_ids=true | all-gather | bytes 147456 | tf_op jit(solution)/shard_map/all_gather | solution.py:75
  52.4 5.6 %all-to-all-start = ((f32[1,128,1024]{2,0,1:T(1,128)}), f32[1,128,1024]{2,0,1:T(1,128)S(1)}, u32[]{:S(2)}, u32[]{:S(2)}) async-start(f32[1,128,1024]{2,0,1:T(1,128)} %copy.63), calls=%async_computation | async-start | bytes 1048576 | tf_op jit(solution)/shard_map/all_to_all | solution.py:94
  59.5 2.2 %fusion.15 = f32[16,16,1024]{2,0,1:T(8,128)} fusion(f32[8,16,1024]{2,1,0:T(8,128)S(1)} %bitcast.138), kind=kOutput, calls=%fused_computation.44 | convolution fusion | flops 25167616 | bytes 1572864 | tf_op jit(solution)/shard_map/kq,qgc->kgc/dot_general | solution.py:18
  61.7 6.6 %all-to-all-done = f32[1,128,1024]{2,0,1:T(1,128)S(1)} async-done(((f32[1,128,1024]{2,0,1:T(1,128)}), f32[1,128,1024]{2,0,1:T(1,128)S(1)}, u32[]{:S(2)}, u32[]{:S(2)}) %all-to-all-start) | async-done | bytes 524320 | tf_op jit(solution)/shard_map/all_to_all | solution.py:94
  69.7 2.5 %fusion.9 = (bf16[1,16,16,1024]{3,1,2,0:T(8,128)(2,1)S(1)}, bf16[1,16,16,1024]{3,1,2,0:T(8,128)(2,1)S(1)}, bf16[1,16,16,1024]{3,1,2,0:T(8,128)(2,1)S(1)}, bf16[1,16,16,1024]{3,1,2,0:T(8,128)(2,1)}) fusion(f32[16,16,1024]{2,0,1:T(8,128)S(1)} %convolution_negate_fusion, f32[16,16,1024]{2,0,1:T(8,128)S(1)} %copy-done.3, f32[16,16]{0,1:T(8,128)S(1)} %get-tuple-element.27, ...), kind=kOutput, calls=%fused_computation.35 | convolution fusion | flops 29361920 | bytes 5769216 | tf_op jit(solution)/shard_map/kq,qgc->kgc/dot_general | solution.py:18
  72.2 1.5 copy.74
  73.8 3.7 %all-to-all-start.3 = ((bf16[2,16,16,1024]{3,2,0,1:T(8,128)(2,1)}), bf16[2,16,16,1024]{3,2,0,1:T(8,128)(2,1)S(1)}, u32[]{:S(2)}, u32[]{:S(2)}) async-start(bf16[2,16,16,1024]{3,2,0,1:T(8,128)(2,1)} %copy.74), calls=%async_computation.3 | async-start | bytes 2097152 | tf_op jit(solution)/shard_map/all_to_all | solution.py:103
  78.6 1.6 copy.66
  80.2 14.4 %all-to-all-done.3 = bf16[2,16,16,1024]{3,2,0,1:T(8,128)(2,1)S(1)} async-done(((bf16[2,16,16,1024]{3,2,0,1:T(8,128)(2,1)}), bf16[2,16,16,1024]{3,2,0,1:T(8,128)(2,1)S(1)}, u32[]{:S(2)}, u32[]{:S(2)}) %all-to-all-start.3) | async-done | bytes 1048608 | tf_op jit(solution)/shard_map/all_to_all | solution.py:103
  95.6 3.7 %all-to-all-start.1 = ((bf16[2,16,16,1024]{3,2,0,1:T(8,128)(2,1)}), bf16[2,16,16,1024]{3,2,0,1:T(8,128)(2,1)S(1)}, u32[]{:S(2)}, u32[]{:S(2)}) async-start(bf16[2,16,16,1024]{3,2,0,1:T(8,128)(2,1)} %copy.66), calls=%async_computation.1 | async-start | bytes 2097152 | tf_op jit(solution)/shard_map/all_to_all | solution.py:100
  101.9 1.8 fusion.37
  103.7 1.9 convolution_subtract_fusion.1
  105.6 15.1 %all-to-all-done.1 = bf16[2,16,16,1024]{3,2,0,1:T(8,128)(2,1)S(1)} async-done(((bf16[2,16,16,1024]{3,2,0,1:T(8,128)(2,1)}), bf16[2,16,16,1024]{3,2,0,1:T(8,128)(2,1)S(1)}, u32[]{:S(2)}, u32[]{:S(2)}) %all-to-all-start.1) | async-done | bytes 1048608 | tf_op jit(solution)/shard_map/all_to_all | solution.py:100
  130.0 1.6 subtract_bitcast_fusion
  131.6 1.5 pad_maximum_fusion
  133.0 4.2 %copy.84 = f32[2,2,128,1024]{3,1,0,2:T(2,128)} copy(f32[2,2,128,1024]{2,3,1,0:T(8,128)} %pad_maximum_fusion) | data formatting | bytes 4194304 | tf_op jit(solution)/shard_map/stack | solution.py:117
  137.2 50.2 %all_to_all.78 = f32[2,2,128,1024]{3,1,0,2:T(2,128)S(1)} all-to-all(f32[2,2,128,1024]{3,1,0,2:T(2,128)} %copy.84), channel_id=1, replica_groups=mesh['group'=2,'seq'=8,'chan'=2] {'seq'}, dimensions={2} | all-to-all | bytes 4194304 | tf_op jit(solution)/shard_map/all_to_all | solution.py:120
  190.6 1.7 squeeze.36
  192.3 2.0 fusion.71
  194.3 1.8 copy.87
  196.1 1.9 squeeze.37
  199.0 17.3 %all_to_all.79 = f32[8,16,1024]{2,1,0:T(8,128)S(1)} all-to-all(f32[8,16,1024]{2,1,0:T(8,128)S(1)} %copy.88), channel_id=1, replica_groups=mesh['group'=2,'seq'=8,'chan'=2] {'seq'}, dimensions={0} | all-to-all | bytes 1048576 | tf_op jit(solution)/shard_map/all_to_all | solution.py:124
  (71 shorter events, 27.3 us)
Async XLA Ops:
  0.0 9.6 %copy-start.9 = (s32[8,4]{0,1:T(4,128)S(1)}, s32[8,4]{0,1:T(4,128)}, u32[]{:S(2)}) copy-start(s32[8,4]{0,1:T(4,128)} %param.10) | copy-start | bytes 388
  0.0 9.7 %copy-start.7 = (bf16[1,8,1024]{2,1,0:T(8,128)(2,1)S(1)}, bf16[1,8,1024]{2,1,0:T(8,128)(2,1)}, u32[]{:S(2)}) copy-start(bf16[1,8,1024]{2,1,0:T(8,128)(2,1)} %param.8) | copy-start | bytes 49156
  0.0 46.9 %copy-start.5 = (bf16[128,3,1024]{2,0,1:T(8,128)(2,1)S(1)}, bf16[128,3,1024]{2,0,1:T(8,128)(2,1)}, u32[]{:S(2)}) copy-start(bf16[128,3,1024]{2,0,1:T(8,128)(2,1)} %param.7) | copy-start | bytes 2359300
  0.0 47.1 %copy-start.10 = (s32[8]{0:T(128)S(1)}, s32[8]{0:T(128)}, u32[]{:S(2)}) copy-start(s32[8]{0:T(128)} %param.9) | copy-start | bytes 100
  2.3 50.1 %all-to-all-start.2 = ((f32[1,128,1024]{2,0,1:T(1,128)}), f32[1,128,1024]{2,0,1:T(1,128)S(1)}, u32[]{:S(2)}, u32[]{:S(2)}) async-start(f32[1,128,1024]{2,0,1:T(1,128)} %broadcast_in_dim.12), calls=%async_computation.2 | async-start | bytes 1048576 | tf_op jit(solution)/shard_map/all_to_all | solution.py:97
  9.7 39.2 %copy-start.6 = (f32[3,3,1024]{2,1,0:T(4,128)S(1)}, f32[3,3,1024]{2,1,0:T(4,128)}, u32[]{:S(2)}) copy-start(f32[3,3,1024]{2,1,0:T(4,128)} %param.11) | copy-start | bytes 110596
  47.6 2.7 %collective-permute-start = (bf16[2,3,1024]{2,0,1:T(2,128)(2,1)S(1)}, bf16[2,3,1024]{2,0,1:T(2,128)(2,1)S(1)}, u32[]{:S(2)}, u32[]{:S(2)}) collective-permute-start(bf16[2,3,1024]{2,0,1:T(2,128)(2,1)S(1)} %fusion.58), channel_id=1, source_target_pairs={{0,2},{2,4},{4,6},{6,8},{8,10},{10,12},{12,14},{1,3},{3,5},{5,7},{... | collective-permute-start | bytes 36872 | tf_op jit(solution)/shard_map/ppermute | solution.py:14
  52.4 15.9 %all-to-all-start = ((f32[1,128,1024]{2,0,1:T(1,128)}), f32[1,128,1024]{2,0,1:T(1,128)S(1)}, u32[]{:S(2)}, u32[]{:S(2)}) async-start(f32[1,128,1024]{2,0,1:T(1,128)} %copy.63), calls=%async_computation | async-start | bytes 1048576 | tf_op jit(solution)/shard_map/all_to_all | solution.py:94
  68.4 1.3 copy-start.3
  73.8 20.9 %all-to-all-start.3 = ((bf16[2,16,16,1024]{3,2,0,1:T(8,128)(2,1)}), bf16[2,16,16,1024]{3,2,0,1:T(8,128)(2,1)S(1)}, u32[]{:S(2)}, u32[]{:S(2)}) async-start(bf16[2,16,16,1024]{3,2,0,1:T(8,128)(2,1)} %copy.74), calls=%async_computation.3 | async-start | bytes 2097152 | tf_op jit(solution)/shard_map/all_to_all | solution.py:103
  94.6 1.0 copy-start
  95.6 25.0 %all-to-all-start.1 = ((bf16[2,16,16,1024]{3,2,0,1:T(8,128)(2,1)}), bf16[2,16,16,1024]{3,2,0,1:T(8,128)(2,1)S(1)}, u32[]{:S(2)}, u32[]{:S(2)}) async-start(bf16[2,16,16,1024]{3,2,0,1:T(8,128)(2,1)} %copy.66), calls=%async_computation.1 | async-start | bytes 2097152 | tf_op jit(solution)/shard_map/all_to_all | solution.py:100
  122.7 1.2 copy-start.1
  123.9 1.2 copy-start.2
  192.3 2.0 copy-start.4
  198.7 17.6 %copy-start.8 = (f32[1024]{0:T(1024)S(1)}, f32[1024]{0:T(1024)}, u32[]{:S(2)}) copy-start(f32[1024]{0:T(1024)} %param.13) | copy-start | bytes 12292
where the time goes:
time: 218 us; the launch traced here: 217 us
  blocking collectives  105 us (48%)
  waiting for transfers between devices  37.5 us (17%)
  matrix products  24.5 us (11%)
  local copies, waits for them, and re-layouts  23.8 us (11%)
  starting transfers between devices  21.6 us (10%)
  other arithmetic  4.82 us (2%)
    all_to_all x1, blocking collectives, body(): lax.all_to_all(turned, 'seq', split_axis=2, concat_axis=1, tiled=True)  50.2 us
    all_gather x1, blocking collectives, body(): shards = lax.all_gather(library, 'seq', axis=0, tiled=True)  37.2 us
    dot_general x18, matrix products, exact_dot(): return jnp.einsum(pattern, matrix, tensor, precision=lax.Precision.HIGHEST)  24.2 us
    all_to_all x1, blocking collectives, body(): lax.all_to_all(positions, 'seq', split_axis=0, concat_axis=1, tiled=True)[0]  17.3 us
    all_to_all x1, waiting for transfers between devices, body(): lax.all_to_all(spread_signal.astype(jnp.bfloat16), 'seq', split_axis=1, c...  15.1 us
    all_to_all x1, waiting for transfers between devices, body(): lax.all_to_all(spread_taps.astype(jnp.bfloat16), 'seq', split_axis=1, con...  14.4 us
    all_to_all x1, starting transfers between devices, body(): lax.all_to_all(long_filter[None], 'seq', split_axis=1, concat_axis=0, til...  7.29 us
    all_to_all x1, waiting for transfers between devices, body(): lax.all_to_all(signal[None], 'seq', split_axis=1, concat_axis=0, tiled=True)  6.61 us
  transfers between devices with their start and end apart: 5, of which 4 were waited for; matrix products, arithmetic and copies ran while one was open for 7% of the time, Pallas kernels for 0%

commit v1 on v0

--- a/solution.py
+++ b/solution.py
@@ -91,7 +91,12 @@
     gating = shortened[:, 0]
     signal = shortened[:, 1] * shortened[:, 2]
     spread_signal = to_modes(
-        lax.all_to_all(signal[None], "seq", split_axis=1, concat_axis=0, tiled=True)
+        jnp.concatenate(
+            lax.all_to_all(
+                jnp.stack(jnp.split(signal[None], lax.axis_size("seq"), axis=1)), "seq", 0, 0
+            ),
+            axis=0,
+        )
     )
     spread_taps = to_modes(
         lax.all_to_all(long_filter[None], "seq", split_axis=1, concat_axis=0, tiled=True)

time: 218 us -> 208 us (0.954)
  blocking collectives: 105 us -> 79.5 us
  waiting for transfers between devices: 37.5 us -> 44.1 us
  local copies, waits for them, and re-layouts: 23.8 us -> 27.8 us
  starting transfers between devices: 21.6 us -> 24.2 us
    all_to_all x1, blocking collectives: 50.2 us -> 33.1 us  [body(): lax.all_to_all(turned, 'seq', split_axis=2, concat_axis=1, tiled=True)]
    all_to_all x1, waiting for transfers between devices: 14.4 us -> 21.1 us  [body(): lax.all_to_all(spread_taps.astype(jnp.bfloat16), 'seq', split_axis=1, con...]
    unnamed x25, local copies, waits for them, and re-layouts: 1.87 us -> 6.8 us
    all_to_all x1, waiting for transfers between devices: 0.01 us -> 4.91 us  [body(): lax.all_to_all(long_filter[None], 'seq', split_axis=1, concat_axis=0, til...]
    all_to_all x1, waiting for transfers between devices: 15.1 us -> 10.2 us  [body(): lax.all_to_all(spread_signal.astype(jnp.bfloat16), 'seq', split_axis=1, c...]
    all_gather x1, blocking collectives: 37.2 us -> 32.7 us  [body(): shards = lax.all_gather(library, 'seq', axis=0, tiled=True)]
    all_to_all x1, blocking collectives: 17.3 us -> 13.8 us  [body(): lax.all_to_all(positions, 'seq', split_axis=0, concat_axis=1, tiled=True)[0]]
    all_to_all x1, starting transfers between devices: 7.29 us -> 4.54 us  [body(): lax.all_to_all(long_filter[None], 'seq', split_axis=1, concat_axis=0, til...]
  transfers between devices with their start and end apart: 5 -> 5, of which waited for: 4 -> 4; matrix products, arithmetic and copies ran while one was open for 7% -> 9% of each run, Pallas kernels for 0% -> 0%
where the time goes in v1:
time: 208 us; the launch traced here: 207 us
  blocking collectives  79.5 us (38%)
  waiting for transfers between devices  44.1 us (21%)
  local copies, waits for them, and re-layouts  27.8 us (13%)
  matrix products  24.4 us (12%)
  starting transfers between devices  24.2 us (12%)
  other arithmetic  6.42 us (3%)
    all_to_all x1, blocking collectives, body(): lax.all_to_all(turned, 'seq', split_axis=2, concat_axis=1, tiled=True)  33.1 us
    all_gather x1, blocking collectives, body(): shards = lax.all_gather(library, 'seq', axis=0, tiled=True)  32.7 us
    dot_general x18, matrix products, exact_dot(): return jnp.einsum(pattern, matrix, tensor, precision=lax.Precision.HIGHEST)  24.2 us
    all_to_all x1, waiting for transfers between devices, body(): lax.all_to_all(spread_taps.astype(jnp.bfloat16), 'seq', split_axis=1, con...  21.1 us
    all_to_all x1, blocking collectives, body(): lax.all_to_all(positions, 'seq', split_axis=0, concat_axis=1, tiled=True)[0]  13.8 us
    all_to_all x1, waiting for transfers between devices, body(): lax.all_to_all(spread_signal.astype(jnp.bfloat16), 'seq', split_axis=1, c...  10.2 us
    all_to_all x1, waiting for transfers between devices, body(): lax.all_to_all(jnp.stack(jnp.split(signal[None], lax.axis_size('seq'), ax...  7.84 us
    all_to_all x1, starting transfers between devices, body(): lax.all_to_all(jnp.stack(jnp.split(signal[None], lax.axis_size('seq'), ax...  7.18 us
  transfers between devices with their start and end apart: 5, of which 4 were waited for; matrix products, arithmetic and copies ran while one was open for 9% of the time, Pallas kernels for 0%

profile of v1, /device:TPU:0, one launch (start us, length us, event | category | flops | bytes accessed | tf_op | source)
XLA Modules:
  0.0 206.8 jit_solution(16063340886157073671)
XLA Ops:
  0.8 32.7 %all_gather.3 = bf16[8,8,1024]{2,1,0:T(8,128)(2,1)S(1)} all-gather(bf16[1,8,1024]{2,1,0:T(8,128)(2,1)} %param.8), channel_id=1, replica_groups=mesh['group'=2,'seq'=8,'chan'=2] {'seq'}, dimensions={0}, use_global_device_ids=true | all-gather | bytes 147456 | tf_op jit(solution)/shard_map/all_gather | solution.py:75
  36.8 3.4 %collective-permute-start = (bf16[2,3,1024]{2,0,1:T(2,128)(2,1)S(1)}, bf16[2,3,1024]{2,0,1:T(2,128)(2,1)S(1)}, u32[]{:S(2)}, u32[]{:S(2)}) collective-permute-start(bf16[2,3,1024]{2,0,1:T(2,128)(2,1)S(1)} %fusion.68), channel_id=1, source_target_pairs={{0,2},{2,4},{4,6},{6,8},{8,10},{10,12},{12,14},{1,3},{3,5},{5,7},{... | collective-permute-start | bytes 36872 | tf_op jit(solution)/shard_map/ppermute | solution.py:14
  41.4 4.5 %all-to-all-start.2 = ((f32[1,128,1024]{2,0,1:T(1,128)}), f32[1,128,1024]{2,0,1:T(1,128)S(1)}, u32[]{:S(2)}, u32[]{:S(2)}) async-start(f32[1,128,1024]{2,0,1:T(1,128)} %broadcast_in_dim.12), calls=%async_computation.2 | async-start | bytes 1048576 | tf_op jit(solution)/shard_map/all_to_all | solution.py:102
  51.7 4.9 %all-to-all-done.2 = f32[1,128,1024]{2,0,1:T(1,128)S(1)} async-done(((f32[1,128,1024]{2,0,1:T(1,128)}), f32[1,128,1024]{2,0,1:T(1,128)S(1)}, u32[]{:S(2)}, u32[]{:S(2)}) %all-to-all-start.2) | async-done | bytes 524320 | tf_op jit(solution)/shard_map/all_to_all | solution.py:102
  56.6 7.2 %all-to-all-start = ((f32[8,1,16,1024]{3,2,1,0:T(8,128)}), f32[8,1,16,1024]{3,2,1,0:T(8,128)S(1)}, u32[]{:S(2)}, u32[]{:S(2)}) async-start(f32[8,1,16,1024]{3,2,1,0:T(8,128)} %fusion.27), calls=%async_computation | async-start | bytes 1048576 | tf_op jit(solution)/shard_map/all_to_all | solution.py:95
  64.1 2.2 %convolution_negate_fusion = f32[16,16,1024]{2,0,1:T(8,128)} fusion(f32[8,16,1024]{2,1,0:T(8,128)S(1)} %bitcast.173), kind=kOutput, calls=%fused_computation.2 | convolution fusion | flops 25429760 | bytes 1572864 | tf_op jit(solution)/shard_map/kq,qgc->kgc/dot_general | solution.py:18
  66.3 7.8 %all-to-all-done = f32[8,1,16,1024]{3,2,1,0:T(8,128)S(1)} async-done(((f32[8,1,16,1024]{3,2,1,0:T(8,128)}), f32[8,1,16,1024]{3,2,1,0:T(8,128)S(1)}, u32[]{:S(2)}, u32[]{:S(2)}) %all-to-all-start) | async-done | bytes 524320 | tf_op jit(solution)/shard_map/all_to_all | solution.py:95
  76.5 2.4 %fusion.9 = (bf16[1,16,16,1024]{3,1,2,0:T(8,128)(2,1)S(1)}, bf16[1,16,16,1024]{3,1,2,0:T(8,128)(2,1)S(1)}, bf16[1,16,16,1024]{3,1,2,0:T(8,128)(2,1)S(1)}, bf16[1,16,16,1024]{3,1,2,0:T(8,128)(2,1)}) fusion(f32[16,16,1024]{2,0,1:T(8,128)S(1)} %copy-done.3, f32[16,16]{0,1:T(8,128)S(1)} %get-tuple-element.27, f32[16,16]{0,1:T(8,128)S(1)} %get-tuple-element.26, ...), kind=kOutput, calls=%fused_computation.35 | convolution fusion | flops 29361920 | bytes 5769216 | tf_op jit(solution)/shard_map/kq,qgc->kgc/dot_general | solution.py:18
  79.1 1.5 copy.73
  80.6 3.7 %all-to-all-start.3 = ((bf16[2,16,16,1024]{3,2,0,1:T(8,128)(2,1)}), bf16[2,16,16,1024]{3,2,0,1:T(8,128)(2,1)S(1)}, u32[]{:S(2)}, u32[]{:S(2)}) async-start(bf16[2,16,16,1024]{3,2,0,1:T(8,128)(2,1)} %copy.73), calls=%async_computation.3 | async-start | bytes 2097152 | tf_op jit(solution)/shard_map/all_to_all | solution.py:108
  85.5 1.6 copy.65
  87.0 21.1 %all-to-all-done.3 = bf16[2,16,16,1024]{3,2,0,1:T(8,128)(2,1)S(1)} async-done(((bf16[2,16,16,1024]{3,2,0,1:T(8,128)(2,1)}), bf16[2,16,16,1024]{3,2,0,1:T(8,128)(2,1)S(1)}, u32[]{:S(2)}, u32[]{:S(2)}) %all-to-all-start.3) | async-done | bytes 1048608 | tf_op jit(solution)/shard_map/all_to_all | solution.py:108
  109.1 5.4 %all-to-all-start.1 = ((bf16[2,16,16,1024]{3,2,0,1:T(8,128)(2,1)}), bf16[2,16,16,1024]{3,2,0,1:T(8,128)(2,1)S(1)}, u32[]{:S(2)}, u32[]{:S(2)}) async-start(bf16[2,16,16,1024]{3,2,0,1:T(8,128)(2,1)} %copy.65), calls=%async_computation.1 | async-start | bytes 2097152 | tf_op jit(solution)/shard_map/all_to_all | solution.py:105
  117.1 1.8 fusion.47
  118.9 1.9 convolution_subtract_fusion.1
  120.7 10.2 %all-to-all-done.1 = bf16[2,16,16,1024]{3,2,0,1:T(8,128)(2,1)S(1)} async-done(((bf16[2,16,16,1024]{3,2,0,1:T(8,128)(2,1)}), bf16[2,16,16,1024]{3,2,0,1:T(8,128)(2,1)S(1)}, u32[]{:S(2)}, u32[]{:S(2)}) %all-to-all-start.1) | async-done | bytes 1048608 | tf_op jit(solution)/shard_map/all_to_all | solution.py:105
  140.3 1.6 subtract_bitcast_fusion
  143.3 4.2 %copy.83 = f32[2,2,128,1024]{3,1,0,2:T(2,128)} copy(f32[2,2,128,1024]{2,3,1,0:T(8,128)} %pad_maximum_fusion) | data formatting | bytes 4194304 | tf_op jit(solution)/shard_map/stack | solution.py:122
  147.5 33.1 %all_to_all.71 = f32[2,2,128,1024]{3,1,0,2:T(2,128)S(1)} all-to-all(f32[2,2,128,1024]{3,1,0,2:T(2,128)} %copy.83), channel_id=1, replica_groups=mesh['group'=2,'seq'=8,'chan'=2] {'seq'}, dimensions={2} | all-to-all | bytes 4194304 | tf_op jit(solution)/shard_map/all_to_all | solution.py:125
  183.8 1.7 squeeze.36
  185.5 2.0 fusion.81
  187.4 1.8 copy.86
  189.2 1.9 squeeze.37
  192.2 13.8 %all_to_all.72 = f32[8,16,1024]{2,1,0:T(8,128)S(1)} all-to-all(f32[8,16,1024]{2,1,0:T(8,128)S(1)} %copy.87), channel_id=1, replica_groups=mesh['group'=2,'seq'=8,'chan'=2] {'seq'}, dimensions={0} | all-to-all | bytes 1048576 | tf_op jit(solution)/shard_map/all_to_all | solution.py:129
  (71 shorter events, 34.1 us)
Async XLA Ops:
  0.8 39.4 %copy-start.5 = (f32[128,1024]{1,0:T(8,128)S(1)}, f32[128,1024]{1,0:T(8,128)}, u32[]{:S(2)}) copy-start(f32[128,1024]{1,0:T(8,128)} %param.12) | copy-start | bytes 1572868
  36.8 9.2 %copy-start.6 = (f32[3,3,1024]{2,1,0:T(4,128)S(1)}, f32[3,3,1024]{2,1,0:T(4,128)}, u32[]{:S(2)}) copy-start(f32[3,3,1024]{2,1,0:T(4,128)} %param.11) | copy-start | bytes 110596
  36.8 9.1 %collective-permute-start = (bf16[2,3,1024]{2,0,1:T(2,128)(2,1)S(1)}, bf16[2,3,1024]{2,0,1:T(2,128)(2,1)S(1)}, u32[]{:S(2)}, u32[]{:S(2)}) collective-permute-start(bf16[2,3,1024]{2,0,1:T(2,128)(2,1)S(1)} %fusion.68), channel_id=1, source_target_pairs={{0,2},{2,4},{4,6},{6,8},{8,10},{10,12},{12,14},{1,3},{3,5},{5,7},{... | collective-permute-start | bytes 36872 | tf_op jit(solution)/shard_map/ppermute | solution.py:14
  41.4 15.2 %all-to-all-start.2 = ((f32[1,128,1024]{2,0,1:T(1,128)}), f32[1,128,1024]{2,0,1:T(1,128)S(1)}, u32[]{:S(2)}, u32[]{:S(2)}) async-start(f32[1,128,1024]{2,0,1:T(1,128)} %broadcast_in_dim.12), calls=%async_computation.2 | async-start | bytes 1048576 | tf_op jit(solution)/shard_map/all_to_all | solution.py:102
  56.6 17.5 %all-to-all-start = ((f32[8,1,16,1024]{3,2,1,0:T(8,128)}), f32[8,1,16,1024]{3,2,1,0:T(8,128)S(1)}, u32[]{:S(2)}, u32[]{:S(2)}) async-start(f32[8,1,16,1024]{3,2,1,0:T(8,128)} %fusion.27), calls=%async_computation | async-start | bytes 1048576 | tf_op jit(solution)/shard_map/all_to_all | solution.py:95
  74.1 2.4 %copy-start.3 = (f32[16,16,1024]{2,0,1:T(8,128)S(1)}, f32[16,16,1024]{2,0,1:T(8,128)}, u32[]{:S(2)}) copy-start(f32[16,16,1024]{2,0,1:T(8,128)} %convolution_negate_fusion) | copy-start | bytes 3145732
  80.6 27.5 %all-to-all-start.3 = ((bf16[2,16,16,1024]{3,2,0,1:T(8,128)(2,1)}), bf16[2,16,16,1024]{3,2,0,1:T(8,128)(2,1)S(1)}, u32[]{:S(2)}, u32[]{:S(2)}) async-start(bf16[2,16,16,1024]{3,2,0,1:T(8,128)(2,1)} %copy.73), calls=%async_computation.3 | async-start | bytes 2097152 | tf_op jit(solution)/shard_map/all_to_all | solution.py:108
  108.2 1.0 copy-start
  109.1 21.8 %all-to-all-start.1 = ((bf16[2,16,16,1024]{3,2,0,1:T(8,128)(2,1)}), bf16[2,16,16,1024]{3,2,0,1:T(8,128)(2,1)S(1)}, u32[]{:S(2)}, u32[]{:S(2)}) async-start(bf16[2,16,16,1024]{3,2,0,1:T(8,128)(2,1)} %copy.65), calls=%async_computation.1 | async-start | bytes 2097152 | tf_op jit(solution)/shard_map/all_to_all | solution.py:105
  133.0 1.2 copy-start.1
  134.2 1.2 copy-start.2
  185.5 2.0 copy-start.4
  191.8 14.1 %copy-start.7 = (f32[1024]{0:T(1024)S(1)}, f32[1024]{0:T(1024)}, u32[]{:S(2)}) copy-start(f32[1024]{0:T(1024)} %param.13) | copy-start | bytes 12292
